TPU v7x, 32 devices: a whole 2x2x4 slice. The times are simulated.
32 devices in a mesh: clips: 2 (over y), tm: 4 (over x, core), rows: 4 (over z).
Axes of the slice: x: 2, y: 2, z: 4, core: 2. Of those that a mesh axis runs over, the one named last changes fastest.
Arguments:
- segment_input: bfloat16 [4, 8, 4, 32, 384], P('clips', 'tm', 'rows'), parts along dimension 0, may hold values from -6 to 6
- inner_input: bfloat16 [4, 8, 4, 32, 384], P('clips', 'tm', 'rows'), parts along dimension 0, may hold values from -6 to 6
- lengths: int32 [4, 4], P('clips', 'tm'), parts along dimension 0, may hold values from 1 to 2
- inner_gain: float32 [384], replicated, may hold values from 0.25 to 1.75
- causal_weight: bfloat16 [3, 3, 3, 384, 384], replicated, may hold values from -0.0625 to 0.0625
- causal_bias: float32 [384], replicated, may hold values from -3 to 3
- attention_gain: float32 [384], replicated, may hold values from 0.25 to 1.75
- triple_weight: bfloat16 [384, 1152], replicated, may hold values from -0.4375 to 0.4375
- triple_bias: float32 [1152], replicated, may hold values from -150 to 150
- output_weight: bfloat16 [384, 384], replicated, may hold values from -0.3125 to 0.3125
- output_bias: float32 [384], replicated, may hold values from -3 to 3
Outputs:
- encoded: bfloat16 [4, 8, 4, 32, 384], P('clips', 'tm', 'rows'), parts along dimension 0
There are 2 independent parts, one for each index of `clips`. A program takes and returns all parts, laid end to end along the dimension named above; an argument that names none is the same for every part. Nothing has to cross between parts.
Inputs may be any that keep to these rules, and one draw needn't show every extreme that they name: The valid frames of a clip in a section are that section's first lengths[b, s] frame slots.
All inputs are finite; a program needn't handle non-finite values.
Results may differ from a plain program's by a relative error of at most 0.0062.
Values may be sent and summed in bfloat16 or wider, within the bound.
No kernel may reach another device: no remote copies, remote signals or barrier semaphores. Data moves between devices by JAX's collectives and lax.ppermute only.
A program may use at most 128 MiB of HBM per device.

v0:
```python
import math
import jax
import jax.numpy as jnp
from jax import lax
from jax.sharding import PartitionSpec as P

EPSILON = 1e-06


def prefix(part, axis, combine, identity):
    place = lax.axis_index(axis)
    gathered = jax.tree.map(lambda a: lax.all_gather(a, axis), part)
    state = jax.tree.map(lambda a, e: jnp.zeros_like(a) + jnp.asarray(e, a.dtype), part, identity)

    def one(step, state):
        return combine(
            state, jax.tree.map(lambda a: lax.dynamic_index_in_dim(a, step, 0, False), gathered)
        )

    return lax.fori_loop(0, place, one, state)


def as_sent(x):

    def short(part):
        return part.astype(jnp.bfloat16) if part.dtype == jnp.float32 else part

    return jax.tree.map(short, x)


def with_halo(cells, sides, width):
    for axis, dim in sides:
        count = lax.axis_size(axis)
        ends = count - 1
        head = lax.slice_in_dim(cells, 0, width, axis=dim)
        tail = lax.slice_in_dim(cells, cells.shape[dim] - width, cells.shape[dim], axis=dim)
        cells = jnp.concatenate(
            [
                lax.ppermute(tail, axis, [(i, (i + 1) % count) for i in range(ends)]),
                cells,
                lax.ppermute(head, axis, [((i + 1) % count, i) for i in range(ends)]),
            ],
            axis=dim,
        )
    return cells


def normalize(field, gain):
    widened = field.astype(jnp.float32)
    return widened * lax.rsqrt(jnp.mean(widened * widened, axis=-1, keepdims=True) + EPSILON) * gain


def last_two(extended, counts):
    slot_total = extended.shape[1]
    chosen = []
    for position in range(2):
        target = counts + position
        picked = jnp.zeros_like(extended[:, 0])
        for slot_index in range(slot_total):
            matches = (target == slot_index)[:, None, None, None]
            picked = jnp.where(matches, extended[:, slot_index], picked)
        chosen.append(picked)
    return jnp.stack(chosen, axis=1)


def summarize(activated, counts):
    blanks = jnp.zeros((activated.shape[0], 2) + activated.shape[2:], activated.dtype)
    summary = last_two(jnp.concatenate([blanks, activated], axis=1), counts)
    return (summary, jnp.minimum(counts, 2).astype(jnp.bfloat16))


def join_later(earlier, later):
    early_frames, early_count = earlier
    late_frames, late_count = later
    complete = (late_count > 1.5)[:, None, None, None, None]
    single = (late_count > 0.5)[:, None, None, None, None]
    shifted = jnp.concatenate([early_frames[:, 1:], late_frames[:, 1:]], axis=1)
    frames = jnp.where(complete, late_frames, jnp.where(single, shifted, early_frames))
    total_count = jnp.minimum(early_count + late_count, 2.0).astype(early_count.dtype)
    return (frames, total_count)


def incoming_cache(summary, counts):
    starting = (jnp.zeros_like(summary), jnp.zeros_like(counts))
    combined = prefix((summary, counts), "tm", join_later, starting)
    return combined[0]


def convolve(padded, causal_weight, causal_bias):
    clip_count, slot_total, rows_padded, column_count, channels = padded.shape
    frame_count = slot_total - 2
    row_count = rows_padded - 2
    widened = jnp.pad(padded, ((0, 0), (0, 0), (0, 0), (1, 1), (0, 0)))
    summed = jnp.zeros((clip_count * frame_count * row_count * column_count, channels), jnp.float32)
    for delta_time in range(3):
        for delta_row in range(3):
            window = widened[
                :, delta_time : delta_time + frame_count, delta_row : delta_row + row_count
            ]
            columns = jnp.concatenate(
                [window[:, :, :, delta_col : delta_col + column_count] for delta_col in range(3)],
                axis=-1,
            )
            kernel = causal_weight[delta_time, delta_row].reshape(3 * channels, channels)
            summed = summed + jnp.dot(
                columns.reshape(-1, 3 * channels), kernel, preferred_element_type=jnp.float32
            )
    return summed.reshape(clip_count, frame_count, row_count, column_count, channels) + causal_bias


def attend(normed, triple_weight, triple_bias, output_weight, output_bias):
    frame_count, places, channels = normed.shape
    packed = (
        jnp.dot(normed.reshape(-1, channels), triple_weight, preferred_element_type=jnp.float32)
        + triple_bias
    )
    packed = packed.reshape(frame_count, places, 3 * channels)
    queries = packed[:, :, :channels]
    key_vectors = packed[:, :, channels : 2 * channels]
    values = packed[:, :, 2 * channels :].astype(jnp.bfloat16)
    scores = jnp.einsum(
        "nqc,nkc->nqk", queries, key_vectors, precision=lax.Precision.HIGHEST
    ) / math.sqrt(channels)
    row_max = jnp.max(scores, axis=-1, keepdims=True)
    exponent = jnp.exp(scores - row_max)
    weights = (exponent / jnp.sum(exponent, axis=-1, keepdims=True)).astype(jnp.bfloat16)
    attended = jnp.einsum(
        "nqk,nkc->nqc", weights, values, preferred_element_type=jnp.float32
    ).astype(jnp.bfloat16)
    projected = (
        jnp.dot(attended.reshape(-1, channels), output_weight, preferred_element_type=jnp.float32)
        + output_bias
    )
    return projected.reshape(frame_count, places, channels).astype(jnp.bfloat16)


def body(
    segment_input,
    inner_input,
    lengths,
    inner_gain,
    causal_weight,
    causal_bias,
    attention_gain,
    triple_weight,
    triple_bias,
    output_weight,
    output_bias,
):
    clip_count, frame_count, row_count, column_count, channels = segment_input.shape
    activated = jax.nn.silu(normalize(inner_input, inner_gain)).astype(jnp.bfloat16)
    counts = lengths[:, 0]
    live_mask = (jnp.arange(frame_count, dtype=jnp.int32)[None, :] < counts[:, None]).astype(
        jnp.float32
    )
    carried = incoming_cache(*summarize(activated, counts))
    extended = jnp.concatenate([carried, activated], axis=1)
    padded = with_halo(as_sent(extended), (("rows", 2),), 1).astype(extended.dtype)
    convolved = convolve(padded, causal_weight, causal_bias)
    residual = (segment_input.astype(jnp.float32) + convolved).astype(jnp.bfloat16)
    residual = lax.optimization_barrier(residual)
    normed = normalize(residual, attention_gain).astype(jnp.bfloat16)
    row_devices = lax.axis_size("rows")
    per_device = clip_count * frame_count // row_devices
    grouped = normed.reshape(row_devices, per_device, row_count, column_count, channels)
    portion = lax.all_to_all(grouped, "rows", split_axis=0, concat_axis=2, tiled=True)
    owned = portion.shape[1]
    height = portion.shape[2]
    flat = portion.reshape(owned, height * column_count, channels)
    result = attend(flat, triple_weight, triple_bias, output_weight, output_bias)
    result = result.reshape(1, owned, height, column_count, channels)
    projected = lax.all_to_all(result, "rows", split_axis=2, concat_axis=0, tiled=True)
    projected = projected.reshape(clip_count, frame_count, row_count, column_count, channels)
    projected = lax.optimization_barrier(projected)
    summed = residual.astype(jnp.float32) + projected.astype(jnp.float32)
    return (summed * live_mask[:, :, None, None, None]).astype(jnp.bfloat16)


def activate(field, gain):
    return jax.nn.silu(normalize(field, gain)).astype(jnp.bfloat16)


def gathered_body(
    segment_input,
    inner_input,
    lengths,
    inner_gain,
    causal_weight,
    causal_bias,
    attention_gain,
    triple_weight,
    triple_bias,
    output_weight,
    output_bias,
):
    clip_count, frame_count, row_count, column_count, channels = segment_input.shape
    sections = lax.axis_size("tm")
    inner_all = lax.all_gather(inner_input, "rows", axis=2, tiled=True)
    segment_all = lax.all_gather(segment_input, "rows", axis=2, tiled=True)
    counts = lengths[:, 0]
    wide = (counts > 1)[:, None, None, None]
    last_raw = jnp.where(wide, inner_all[:, frame_count - 1], inner_all[:, 0])
    prev_raw = lax.ppermute(inner_all, "tm", [(i, i + 1) for i in range(sections - 1)])
    prev_counts = lax.ppermute(counts, "tm", [(i, i + 1) for i in range(sections - 1)])
    before_raw = lax.ppermute(last_raw, "tm", [(i, i + 2) for i in range(sections - 2)])
    own = activate(inner_all, inner_gain)
    prev = activate(prev_raw, inner_gain)
    before = activate(before_raw, inner_gain)
    prev_wide = (prev_counts > 1)[:, None, None, None]
    carried = jnp.stack(
        [
            jnp.where(prev_wide, prev[:, frame_count - 2], before),
            jnp.where(prev_wide, prev[:, frame_count - 1], prev[:, 0]),
        ],
        axis=1,
    )
    extended = jnp.concatenate([carried, own], axis=1)
    padded = jnp.pad(extended, ((0, 0), (0, 0), (1, 1), (0, 0), (0, 0)))
    convolved = convolve(padded, causal_weight, causal_bias)
    residual = (segment_all.astype(jnp.float32) + convolved).astype(jnp.bfloat16)
    normed = normalize(residual, attention_gain).astype(jnp.bfloat16)
    height = normed.shape[2]
    frames = clip_count * frame_count
    places = height * column_count
    flat = normed.reshape(frames * places, channels)
    packed = (
        jnp.dot(flat, triple_weight[:, channels:], preferred_element_type=jnp.float32)
        + triple_bias[channels:]
    ).reshape(frames, places, 2 * channels)
    key_vectors = packed[:, :, :channels]
    values = packed[:, :, channels:].astype(jnp.bfloat16)
    start = lax.axis_index("rows") * row_count
    mine = lax.dynamic_slice_in_dim(normed, start, row_count, axis=2)
    queries = (
        jnp.dot(
            mine.reshape(-1, channels),
            triple_weight[:, :channels],
            preferred_element_type=jnp.float32,
        )
        + triple_bias[:channels]
    ).reshape(frames, row_count * column_count, channels)
    scores = jnp.einsum(
        "nqc,nkc->nqk", queries, key_vectors, precision=lax.Precision.HIGHEST
    ) / math.sqrt(channels)
    row_max = jnp.max(scores, axis=-1, keepdims=True)
    exponent = jnp.exp(scores - row_max)
    weights = (exponent / jnp.sum(exponent, axis=-1, keepdims=True)).astype(jnp.bfloat16)
    attended = jnp.einsum(
        "nqk,nkc->nqc", weights, values, preferred_element_type=jnp.float32
    ).astype(jnp.bfloat16)
    projected = (
        jnp.dot(attended.reshape(-1, channels), output_weight, preferred_element_type=jnp.float32)
        + output_bias
    ).astype(jnp.bfloat16)
    projected = projected.reshape(clip_count, frame_count, row_count, column_count, channels)
    residual_mine = lax.dynamic_slice_in_dim(residual, start, row_count, axis=2)
    live_mask = (jnp.arange(frame_count, dtype=jnp.int32)[None, :] < counts[:, None]).astype(
        jnp.float32
    )
    summed = residual_mine.astype(jnp.float32) + projected.astype(jnp.float32)
    return (summed * live_mask[:, :, None, None, None]).astype(jnp.bfloat16)


GATHER_LIMIT = 1 << 22


def chosen_body(segment_input, inner_input, *rest):
    gathered = inner_input.size * inner_input.dtype.itemsize * lax.axis_size("rows")
    if gathered <= GATHER_LIMIT:
        return gathered_body(segment_input, inner_input, *rest)
    return body(segment_input, inner_input, *rest)


def solution(mesh):
    placed = (
        P("clips", "tm", "rows", None, None),
        P("clips", "tm", "rows", None, None),
        P("clips", "tm"),
        P(),
        P(),
        P(),
        P(),
        P(),
        P(),
        P(),
        P(),
    )
    return jax.shard_map(
        chosen_body,
        mesh=mesh,
        in_specs=placed,
        out_specs=P("clips", "tm", "rows", None, None),
        check_vma=False,
    )
```

profile of v0, /device:TPU:0, one launch (start us, length us, event | category | flops | bytes accessed | tf_op | source)
XLA Modules:
  0.0 70.2 jit_solution(4416258537205051209)
XLA Ops:
  0.0 16.6 %all_gather.7 = bf16[2,2,4,32,384]{4,3,2,1,0:T(8,128)(2,1)S(1)} all-gather(bf16[2,2,1,32,384]{4,3,2,1,0:T(8,128)(2,1)} %param.12), channel_id=1, replica_groups=mesh['clips'=2,'tm'=4,'rows'=4] {'rows'}, dimensions={2}, use_global_device_ids=true | all-gather | bytes 491520 | tf_op jit(solution)/shard_map/all_gather | solution.py:198
  16.6 0.8 %copy.33 = bf16[2,2,4,32,384]{4,3,2,0,1:T(8,128)(2,1)} copy(bf16[2,2,4,32,384]{4,3,2,1,0:T(8,128)(2,1)S(1)} %all_gather.7) | data formatting | bytes 786432 | tf_op jit(solution)/shard_map/all_gather | solution.py:198
  17.4 1.3 %collective-permute-start.1 = (bf16[2,2,4,32,384]{4,3,2,0,1:T(8,128)(2,1)}, bf16[2,2,4,32,384]{4,3,2,0,1:T(8,128)(2,1)S(1)}, u32[]{:S(2)}, u32[]{:S(2)}) collective-permute-start(bf16[2,2,4,32,384]{4,3,2,0,1:T(8,128)(2,1)} %copy.33), channel_id=1, source_target_pairs={{0,4},{4,8},{8,12},{1,5},{5,9},{9,13},{2,6},{6,10},{10,14},{3,7},{... | collective-permute-start | bytes 1179656 | tf_op jit(solution)/shard_map/ppermute | solution.py:203
  18.7 0.7 broadcast_compare_fusion
  19.4 0.8 %fusion.42 = bf16[2,4,32,384]{3,2,1,0:T(8,128)(2,1)} fusion(pred[2]{0:T(512)(128)(4,1)S(1)} %broadcast_compare_fusion, bf16[2,2,4,32,384]{4,3,2,1,0:T(8,128)(2,1)S(1)} %all_gather.7), kind=kLoop, calls=%fused_computation.98 | loop fusion | flops 98304 | bytes 589826 | tf_op jit(solution)/shard_map/jit(_where)/select_n | solution.py:202
  20.2 4.0 %collective-permute-start.2 = (bf16[2,4,32,384]{3,2,1,0:T(8,128)(2,1)}, bf16[2,4,32,384]{3,2,1,0:T(8,128)(2,1)S(1)}, u32[]{:S(2)}, u32[]{:S(2)}) collective-permute-start(bf16[2,4,32,384]{3,2,1,0:T(8,128)(2,1)} %fusion.42), channel_id=1, source_target_pairs={{0,8},{4,12},{1,9},{5,13},{2,10},{6,14},{3,11},{7,15},{16,24},{20,... | collective-permute-start | bytes 589832 | tf_op jit(solution)/shard_map/ppermute | solution.py:205
  24.2 1.4 %collective-permute-start = (s32[2]{0:T(128)S(1)}, s32[2]{0:T(128)S(1)}, u32[]{:S(2)}, u32[]{:S(2)}) collective-permute-start(s32[2]{0:T(128)S(1)} %bitcast.102), channel_id=1, source_target_pairs={{0,4},{4,8},{8,12},{1,5},{5,9},{9,13},{2,6},{6,10},{10,14},{3,7},{... | collective-permute-start | bytes 32 | tf_op jit(solution)/shard_map/ppermute | solution.py:204
  25.6 0.2 fusion.20
  25.9 5.4 %fusion.52 = (bf16[1,1,3,384,384]{4,3,2,1,0:T(8,128)(2,1)S(1)}, bf16[1,1,3,384,384]{4,3,2,1,0:T(8,128)(2,1)}, bf16[1,1,3,384,384]{4,3,2,1,0:T(8,128)(2,1)}, bf16...) fusion(bf16[3,3,3,384,384]{4,3,2,1,0:T(8,128)(2,1)} %param.15), kind=kLoop, calls=%fused_computation.119 | loop fusion | bytes 15925248 | tf_op jit(solution)/shard_map/slice | solution.py:104
  31.3 16.0 %all_gather.6 = bf16[2,2,4,32,384]{4,3,2,1,0:T(8,128)(2,1)} all-gather(bf16[2,2,1,32,384]{4,3,2,1,0:T(8,128)(2,1)S(1)} %copy-done.10), channel_id=1, replica_groups=mesh['clips'=2,'tm'=4,'rows'=4] {'rows'}, dimensions={2}, use_global_device_ids=true | all-gather | bytes 491520 | tf_op jit(solution)/shard_map/all_gather | solution.py:199
  47.3 0.4 fusion.26
  47.9 0.2 fusion.12
  48.1 0.3 fusion.19
  48.5 0.2 fusion.45
  48.9 3.5 %pad_slice_fusion.1 = (bf16[2,2,4,32,384]{4,3,2,1,0:T(8,128)(2,1)S(1)}, bf16[2,2,4,32,384]{4,3,2,1,0:T(8,128)(2,1)S(1)}, bf16[2,2,4,32,384]{4,3,2,1,0:T(8,128)(2...) fusion(bf16[2,4,6,32,384]{4,3,2,1,0:T(8,128)(2,1)S(1)} %fusion.6), kind=kLoop, calls=%fused_computation.37 | loop fusion | bytes 9437184 | tf_op jit(solution)/shard_map/slice | solution.py:101
  52.4 0.3 fusion.53
  52.7 0.3 pad_maximum_fusion.1
  53.0 0.9 %copy-done.9 = bf16[1,1,3,384,384]{4,3,2,1,0:T(8,128)(2,1)S(1)} copy-done((bf16[1,1,3,384,384]{4,3,2,1,0:T(8,128)(2,1)S(1)}, bf16[1,1,3,384,384]{4,3,2,1,0:T(8,128)(2,1)}, u32[]{:S(2)}) %copy-start.9) | copy-done | bytes 884760
  53.9 0.8 %fusion.55 = f32[512,384]{1,0:T(8,128)S(1)} fusion(bf16[512,1152]{1,0:T(8,128)(2,1)S(1)} %bitcast.96, bf16[1152,384]{1,0:T(8,128)(2,1)S(1)} %bitcast.97), kind=kOutput, calls=%fused_computation.122 | convolution fusion | flops 452984832 | bytes 2850816 | tf_op jit(solution)/shard_map/dot_general | solution.py:105
  54.7 0.4 pad_maximum_fusion.7
  55.1 0.7 %copy-done.6 = bf16[1,1,3,384,384]{4,3,2,1,0:T(8,128)(2,1)S(1)} copy-done((bf16[1,1,3,384,384]{4,3,2,1,0:T(8,128)(2,1)S(1)}, bf16[1,1,3,384,384]{4,3,2,1,0:T(8,128)(2,1)}, u32[]{:S(2)}) %copy-start.6) | copy-done | bytes 884760
  55.8 0.8 %convolution_add_fusion.8 = f32[512,384]{1,0:T(8,128)S(1)} fusion(f32[512,384]{1,0:T(8,128)S(1)} %fusion.55, bf16[512,1152]{1,0:T(8,128)(2,1)S(1)} %bitcast.80, bf16[1152,384]{1,0:T(8,128)(2,1)S(1)} %bitcast.93), kind=kOutput, calls=%fused_computation.15 | convolution fusion | flops 453181440 | bytes 3637248 | tf_op jit(solution)/shard_map/dot_general | solution.py:105
  56.6 0.4 copy-done.5
  57.0 0.8 %convolution_add_fusion.7 = f32[512,384]{1,0:T(8,128)S(1)} fusion(f32[512,384]{1,0:T(8,128)S(1)} %convolution_add_fusion.8, bf16[512,1152]{1,0:T(8,128)(2,1)S(1)} %bitcast.81, bf16[1152,384]{1,0:T(8,128)(2,1)S(1)} %bitcast.92), kind=kOutput, calls=%fused_computation.14 | convolution fusion | flops 453181440 | bytes 3637248 | tf_op jit(solution)/shard_map/dot_general | solution.py:105
  57.8 0.3 pad_maximum_fusion.4
  58.1 0.9 %copy-done.4 = bf16[1,1,3,384,384]{4,3,2,1,0:T(8,128)(2,1)S(1)} copy-done((bf16[1,1,3,384,384]{4,3,2,1,0:T(8,128)(2,1)S(1)}, bf16[1,1,3,384,384]{4,3,2,1,0:T(8,128)(2,1)}, u32[]{:S(2)}) %copy-start.4) | copy-done | bytes 884760
  59.0 0.8 %convolution_add_fusion.6 = f32[512,384]{1,0:T(8,128)S(1)} fusion(f32[512,384]{1,0:T(8,128)S(1)} %convolution_add_fusion.7, bf16[512,1152]{1,0:T(8,128)(2,1)S(1)} %bitcast.84, bf16[1152,384]{1,0:T(8,128)(2,1)S(1)} %bitcast.91), kind=kOutput, calls=%fused_computation.13 | convolution fusion | flops 453181440 | bytes 3637248 | tf_op jit(solution)/shard_map/dot_general | solution.py:105
  59.8 0.4 copy-done.3
  60.1 0.8 %convolution_add_fusion.5 = f32[512,384]{1,0:T(8,128)S(1)} fusion(f32[512,384]{1,0:T(8,128)S(1)} %convolution_add_fusion.6, bf16[512,1152]{1,0:T(8,128)(2,1)S(1)} %bitcast.79, bf16[1152,384]{1,0:T(8,128)(2,1)S(1)} %bitcast.90), kind=kOutput, calls=%fused_computation.12 | convolution fusion | flops 453181440 | bytes 3637248 | tf_op jit(solution)/shard_map/dot_general | solution.py:105
  60.9 0.4 copy-done.2
  61.3 0.8 %convolution_add_fusion.4 = f32[512,384]{1,0:T(8,128)S(1)} fusion(f32[512,384]{1,0:T(8,128)S(1)} %convolution_add_fusion.5, bf16[512,1152]{1,0:T(8,128)(2,1)S(1)} %bitcast.83, bf16[1152,384]{1,0:T(8,128)(2,1)S(1)} %bitcast.89), kind=kOutput, calls=%fused_computation.11 | convolution fusion | flops 453181440 | bytes 3637248 | tf_op jit(solution)/shard_map/dot_general | solution.py:105
  62.1 0.3 pad_maximum_fusion.6
  62.4 0.9 %copy-done.1 = bf16[1,1,3,384,384]{4,3,2,1,0:T(8,128)(2,1)S(1)} copy-done((bf16[1,1,3,384,384]{4,3,2,1,0:T(8,128)(2,1)S(1)}, bf16[1,1,3,384,384]{4,3,2,1,0:T(8,128)(2,1)}, u32[]{:S(2)}) %copy-start.1) | copy-done | bytes 884760
  63.3 0.8 %convolution_add_fusion.3 = f32[512,384]{1,0:T(8,128)S(1)} fusion(f32[512,384]{1,0:T(8,128)S(1)} %convolution_add_fusion.4, bf16[512,1152]{1,0:T(8,128)(2,1)S(1)} %bitcast.85, bf16[1152,384]{1,0:T(8,128)(2,1)S(1)} %bitcast.88), kind=kOutput, calls=%fused_computation.10 | convolution fusion | flops 453181440 | bytes 3637248 | tf_op jit(solution)/shard_map/dot_general | solution.py:105
  64.1 0.8 %convolution_add_fusion.2 = f32[512,384]{1,0:T(8,128)S(1)} fusion(f32[512,384]{1,0:T(8,128)S(1)} %convolution_add_fusion.3, bf16[512,1152]{1,0:T(8,128)(2,1)S(1)} %bitcast.78, bf16[1152,384]{1,0:T(8,128)(2,1)S(1)} %bitcast.87), kind=kOutput, calls=%fused_computation.9 | convolution fusion | flops 453181440 | bytes 3637248 | tf_op jit(solution)/shard_map/dot_general | solution.py:105
  64.9 0.8 %convolution_add_fusion.1 = f32[512,384]{1,0:T(8,128)S(1)} fusion(f32[512,384]{1,0:T(8,128)S(1)} %convolution_add_fusion.2, bf16[512,1152]{1,0:T(8,128)(2,1)S(1)} %bitcast.82, bf16[1152,384]{1,0:T(8,128)(2,1)S(1)} %bitcast.86), kind=kOutput, calls=%fused_computation.8 | convolution fusion | flops 453181440 | bytes 3637248 | tf_op jit(solution)/shard_map/dot_general | solution.py:105
  65.7 0.1 copy-done.7
  65.9 0.2 fusion.22
  66.1 0.3 copy-done.14
  66.4 0.2 fusion.24
  66.7 0.3 copy-done.8
  66.9 0.6 convolution_add_fusion
  67.5 0.2 convolution_add_fusion.10
  67.7 1.0 %convolution_multiply_fusion = f32[4,32,128]{2,1,0:T(8,128)S(1)} fusion(f32[4,32,384]{2,1,0:T(8,128)S(1)} %bitcast.98, f32[4,128,768]{2,1,0:T(8,128)S(1)} %bitcast.76), kind=kOutput, calls=%fused_computation.35 | convolution fusion | flops 75513856 | bytes 1048576 | tf_op jit(solution)/shard_map/nqc,nkc->nqk/dot_general | solution.py:242
  68.7 0.2 fusion.54
  68.9 0.3 convolution_convert_fusion
  69.2 0.2 fusion.9
  69.4 0.7 %fusion.44 = bf16[2,2,1,32,384]{4,3,2,1,0:T(8,128)(2,1)} fusion(bf16[2,2,1,32,384]{4,3,2,1,0:T(8,128)(2,1)S(1)} %bitcast.101, f32[2,2]{1,0:T(2,128)S(1)} %compare_convert_fusion, bf16[2,2,4,32,384]{4,3,2,1,0:T(8,128)(2,1)S(1)} %get-tuple-element.6, s32[]{:T(128)S(6)} %select_n.18), kind=kLoop, calls=%fused_computation.102 | loop fusion | flops 245760 | bytes 294932 | tf_op jit(solution)/shard_map/convert_element_type | solution.py:261
  (39 shorter events, 0.6 us)
Async XLA Ops:
  0.0 69.2 %copy-start = (bf16[384,384]{1,0:T(8,128)(2,1)S(1)}, bf16[384,384]{1,0:T(8,128)(2,1)}, u32[]{:S(2)}) copy-start(bf16[384,384]{1,0:T(8,128)(2,1)} %param.20) | copy-start | bytes 884740
  0.0 24.2 %copy-start.16 = (s32[2,1]{0,1:T(1,128)S(1)}, s32[2,1]{0,1:T(1,128)}, u32[]{:S(2)}) copy-start(s32[2,1]{0,1:T(1,128)} %param.13) | copy-start | bytes 28
  0.0 25.7 %copy-start.12 = (f32[1152]{0:T(1024)S(1)}, f32[1152]{0:T(1024)}, u32[]{:S(2)}) copy-start(f32[1152]{0:T(1024)} %param.19) | copy-start | bytes 13828
  17.4 30.5 %collective-permute-start.1 = (bf16[2,2,4,32,384]{4,3,2,0,1:T(8,128)(2,1)}, bf16[2,2,4,32,384]{4,3,2,0,1:T(8,128)(2,1)S(1)}, u32[]{:S(2)}, u32[]{:S(2)}) collective-permute-start(bf16[2,2,4,32,384]{4,3,2,0,1:T(8,128)(2,1)} %copy.33), channel_id=1, source_target_pairs={{0,4},{4,8},{8,12},{1,5},{5,9},{9,13},{2,6},{6,10},{10,14},{3,7},{... | collective-permute-start | bytes 1179656 | tf_op jit(solution)/shard_map/ppermute | solution.py:203
  20.2 27.6 %collective-permute-start.2 = (bf16[2,4,32,384]{3,2,1,0:T(8,128)(2,1)}, bf16[2,4,32,384]{3,2,1,0:T(8,128)(2,1)S(1)}, u32[]{:S(2)}, u32[]{:S(2)}) collective-permute-start(bf16[2,4,32,384]{3,2,1,0:T(8,128)(2,1)} %fusion.42), channel_id=1, source_target_pairs={{0,8},{4,12},{1,9},{5,13},{2,10},{6,14},{3,11},{7,15},{16,24},{20,... | collective-permute-start | bytes 589832 | tf_op jit(solution)/shard_map/ppermute | solution.py:205
  24.2 23.5 %collective-permute-start = (s32[2]{0:T(128)S(1)}, s32[2]{0:T(128)S(1)}, u32[]{:S(2)}, u32[]{:S(2)}) collective-permute-start(s32[2]{0:T(128)S(1)} %bitcast.102), channel_id=1, source_target_pairs={{0,4},{4,8},{8,12},{1,5},{5,9},{9,13},{2,6},{6,10},{10,14},{3,7},{... | collective-permute-start | bytes 32 | tf_op jit(solution)/shard_map/ppermute | solution.py:204
  25.9 5.5 %copy-start.10 = (bf16[2,2,1,32,384]{4,3,2,1,0:T(8,128)(2,1)S(1)}, bf16[2,2,1,32,384]{4,3,2,1,0:T(8,128)(2,1)}, u32[]{:S(2)}) copy-start(bf16[2,2,1,32,384]{4,3,2,1,0:T(8,128)(2,1)} %param.11) | copy-start | bytes 294916
  25.9 21.5 %copy-start.11 = (f32[384]{0:T(512)S(1)}, f32[384]{0:T(512)}, u32[]{:S(2)}) copy-start(f32[384]{0:T(512)} %param.14) | copy-start | bytes 4612
  52.7 1.2 %copy-start.9 = (bf16[1,1,3,384,384]{4,3,2,1,0:T(8,128)(2,1)S(1)}, bf16[1,1,3,384,384]{4,3,2,1,0:T(8,128)(2,1)}, u32[]{:S(2)}) copy-start(bf16[1,1,3,384,384]{4,3,2,1,0:T(8,128)(2,1)} %get-tuple-element.14) | copy-start | bytes 2654212
  54.7 1.2 %copy-start.6 = (bf16[1,1,3,384,384]{4,3,2,1,0:T(8,128)(2,1)S(1)}, bf16[1,1,3,384,384]{4,3,2,1,0:T(8,128)(2,1)}, u32[]{:S(2)}) copy-start(bf16[1,1,3,384,384]{4,3,2,1,0:T(8,128)(2,1)} %get-tuple-element.13) | copy-start | bytes 2654212
  55.8 1.2 %copy-start.5 = (bf16[1,1,3,384,384]{4,3,2,1,0:T(8,128)(2,1)S(1)}, bf16[1,1,3,384,384]{4,3,2,1,0:T(8,128)(2,1)}, u32[]{:S(2)}) copy-start(bf16[1,1,3,384,384]{4,3,2,1,0:T(8,128)(2,1)} %get-tuple-element.12) | copy-start | bytes 2654212
  57.8 1.2 %copy-start.4 = (bf16[1,1,3,384,384]{4,3,2,1,0:T(8,128)(2,1)S(1)}, bf16[1,1,3,384,384]{4,3,2,1,0:T(8,128)(2,1)}, u32[]{:S(2)}) copy-start(bf16[1,1,3,384,384]{4,3,2,1,0:T(8,128)(2,1)} %get-tuple-element.11) | copy-start | bytes 2654212
  59.0 1.2 %copy-start.3 = (bf16[1,1,3,384,384]{4,3,2,1,0:T(8,128)(2,1)S(1)}, bf16[1,1,3,384,384]{4,3,2,1,0:T(8,128)(2,1)}, u32[]{:S(2)}) copy-start(bf16[1,1,3,384,384]{4,3,2,1,0:T(8,128)(2,1)} %get-tuple-element.10) | copy-start | bytes 2654212
  60.1 1.2 %copy-start.2 = (bf16[1,1,3,384,384]{4,3,2,1,0:T(8,128)(2,1)S(1)}, bf16[1,1,3,384,384]{4,3,2,1,0:T(8,128)(2,1)}, u32[]{:S(2)}) copy-start(bf16[1,1,3,384,384]{4,3,2,1,0:T(8,128)(2,1)} %get-tuple-element.9) | copy-start | bytes 2654212
  62.1 1.2 %copy-start.1 = (bf16[1,1,3,384,384]{4,3,2,1,0:T(8,128)(2,1)S(1)}, bf16[1,1,3,384,384]{4,3,2,1,0:T(8,128)(2,1)}, u32[]{:S(2)}) copy-start(bf16[1,1,3,384,384]{4,3,2,1,0:T(8,128)(2,1)} %get-tuple-element.8) | copy-start | bytes 2654212
  64.9 1.0 %copy-start.7 = (bf16[2,2,4,32,384]{4,3,2,1,0:T(8,128)(2,1)S(1)}, bf16[2,2,4,32,384]{4,3,2,1,0:T(8,128)(2,1)}, u32[]{:S(2)}) copy-start(bf16[2,2,4,32,384]{4,3,2,1,0:T(8,128)(2,1)} %all_gather.6) | copy-start | bytes 1179652
  64.9 1.0 %copy-start.13 = (f32[384]{0:T(512)S(1)}, f32[384]{0:T(512)}, u32[]{:S(2)}) copy-start(f32[384]{0:T(512)} %param.16) | copy-start | bytes 4612
  65.7 0.7 %copy-start.14 = (f32[384]{0:T(512)S(1)}, f32[384]{0:T(512)}, u32[]{:S(2)}) copy-start(f32[384]{0:T(512)} %param.17) | copy-start | bytes 4612
  65.7 1.2 %copy-start.8 = (bf16[384,1152]{1,0:T(8,128)(2,1)S(1)}, bf16[384,1152]{1,0:T(8,128)(2,1)}, u32[]{:S(2)}) copy-start(bf16[384,1152]{1,0:T(8,128)(2,1)} %param.18) | copy-start | bytes 2654212
  66.6 0.9 %slice-start = ((f32[1152]{0:T(1024)}), f32[384]{0:T(512)S(1)}, s32[]{:S(2)}) async-start(f32[1152]{0:T(1024)} %param.19), calls=%async_computation | async-start | bytes 4096 | tf_op jit(solution)/shard_map/slice | solution.py:240
  67.5 1.7 %copy-start.15 = (f32[384]{0:T(512)S(1)}, f32[384]{0:T(512)}, u32[]{:S(2)}) copy-start(f32[384]{0:T(512)} %param.21) | copy-start | bytes 4612
where the time goes:
time: 70.7 us; the launch traced here: 70.2 us
  blocking collectives  32.6 us (46%)
  local copies, waits for them, and re-layouts  15.4 us (22%)
  matrix products  9.39 us (13%)
  starting transfers between devices  6.7 us (9%)
  other arithmetic  5.64 us (8%)
    all_gather x1, blocking collectives, gathered_body(): inner_all = lax.all_gather(inner_input, 'rows', axis=2, tiled=True)  16.6 us
    all_gather x1, blocking collectives, gathered_body(): segment_all = lax.all_gather(segment_input, 'rows', axis=2, tiled=True)  16 us
    dot_general x9, matrix products, convolve(): jnp.dot(columns.reshape(-1, 3 * channels), kernel, preferred_element_type...  7.15 us
    slice x1, local copies, waits for them, and re-layouts, convolve(): causal_weight[delta_time, delta_row].reshape(3 * channels, channels)  5.45 us
    unnamed x34, local copies, waits for them, and re-layouts  5.33 us
    ppermute x1, starting transfers between devices, gathered_body(): lax.ppermute(last_raw, 'tm', [(i, i + 2) for i in range(sections - 2)])  4 us
    slice x2, local copies, waits for them, and re-layouts, convolve(): window[:, :, :, delta_col:delta_col + column_count]  3.81 us
  transfers between devices with their start and end apart: 3, of which 0 were waited for; matrix products, arithmetic and copies ran while one was open for 11% of the time, Pallas kernels for 0%

commit v1 on v0

--- a/solution.py
+++ b/solution.py
@@ -5,6 +5,23 @@
 from jax.sharding import PartitionSpec as P
 
 EPSILON = 1e-06
+
+
+def joined_along(blocks, dim):
+    blocks = jnp.moveaxis(blocks, 0, dim)
+    shape = blocks.shape
+    return blocks.reshape(*shape[:dim], shape[dim] * shape[dim + 1], *shape[dim + 2 :])
+
+
+def collect(x, axis, dim):
+    length = lax.axis_size(axis)
+    upward = [(i, (i + 1) % length) for i in range(length)]
+    pieces = [x]
+    while len(pieces) < length:
+        pieces.append(lax.ppermute(pieces[-1], axis, upward))
+    place = lax.axis_index(axis)
+    pieces = jnp.stack(pieces)[(place - jnp.arange(length)) % length]
+    return joined_along(pieces, dim)
 
 
 def prefix(part, axis, combine, identity):
@@ -196,7 +213,7 @@
     clip_count, frame_count, row_count, column_count, channels = segment_input.shape
     sections = lax.axis_size("tm")
     inner_all = lax.all_gather(inner_input, "rows", axis=2, tiled=True)
-    segment_all = lax.all_gather(segment_input, "rows", axis=2, tiled=True)
+    segment_all = collect(segment_input, "rows", 2)
     counts = lengths[:, 0]
     wide = (counts > 1)[:, None, None, None]
     last_raw = jnp.where(wide, inner_all[:, frame_count - 1], inner_all[:, 0])

time: 70.7 us -> 76.9 us (1.088)
  blocking collectives: 32.6 us -> 16.6 us
  waiting for transfers between devices: 0.01 us -> 12.9 us
  other arithmetic: 5.64 us -> 10.2 us
  starting transfers between devices: 6.7 us -> 9.36 us
  local copies, waits for them, and re-layouts: 15.4 us -> 16.6 us
    all_gather x1 -> x0, blocking collectives: 16 us -> none  [gathered_body(): segment_all = lax.all_gather(segment_input, 'rows', axis=2, tiled=True)]
    ppermute x0 -> x3, waiting for transfers between devices: none -> 12.9 us  [collect(): pieces.append(lax.ppermute(pieces[-1], axis, upward))]
    ppermute x0 -> x3, starting transfers between devices: none -> 2.18 us  [collect(): pieces.append(lax.ppermute(pieces[-1], axis, upward))]
    gather x0 -> x1, local copies, waits for them, and re-layouts: none -> 1.75 us  [collect(): pieces = jnp.stack(pieces)[(place - jnp.arange(length)) % length]]
    another operation x0 -> x1, other arithmetic: none -> 1.71 us  [collect(): pieces = jnp.stack(pieces)[(place - jnp.arange(length)) % length]]
    unnamed x34, local copies, waits for them, and re-layouts: 5.33 us -> 4.08 us
    convert_element_type x1, other arithmetic: 0.07 us -> 1.24 us  [gathered_body(): (jnp.arange(frame_count, dtype=jnp.int32)[None, :] < counts[:, None]).ast...]
    gt x1, other arithmetic: 0.01 us -> 1.05 us  [gathered_body(): prev_wide = (prev_counts > 1)[:, None, None, None]]
  transfers between devices with their start and end apart: 3 -> 6, of which waited for: 0 -> 2; matrix products, arithmetic and copies ran while one was open for 11% -> 18% of each run, Pallas kernels for 0% -> 0%
where the time goes in v1:
time: 76.9 us; the launch traced here: 76.3 us
  local copies, waits for them, and re-layouts  16.6 us (22%)
  blocking collectives  16.6 us (22%)
  waiting for transfers between devices  12.9 us (17%)
  other arithmetic  10.2 us (13%)
  matrix products  10.1 us (13%)
  starting transfers between devices  9.36 us (12%)
    all_gather x1, blocking collectives, gathered_body(): inner_all = lax.all_gather(inner_input, 'rows', axis=2, tiled=True)  16.6 us
    ppermute x3, waiting for transfers between devices, collect(): pieces.append(lax.ppermute(pieces[-1], axis, upward))  12.9 us
    dot_general x9, matrix products, convolve(): jnp.dot(columns.reshape(-1, 3 * channels), kernel, preferred_element_type...  7.16 us
    slice x1, local copies, waits for them, and re-layouts, convolve(): causal_weight[delta_time, delta_row].reshape(3 * channels, channels)  5.42 us
    unnamed x34, local copies, waits for them, and re-layouts  4.08 us
    ppermute x1, starting transfers between devices, gathered_body(): lax.ppermute(last_raw, 'tm', [(i, i + 2) for i in range(sections - 2)])  4 us
    slice x2, local copies, waits for them, and re-layouts, convolve(): window[:, :, :, delta_col:delta_col + column_count]  3.81 us
    ppermute x3, starting transfers between devices, collect(): pieces.append(lax.ppermute(pieces[-1], axis, upward))  2.18 us
  transfers between devices with their start and end apart: 6, of which 2 were waited for; matrix products, arithmetic and copies ran while one was open for 18% of the time, Pallas kernels for 0%

profile of v1, /device:TPU:0, one launch (start us, length us, event | category | flops | bytes accessed | tf_op | source)
XLA Modules:
  0.0 76.3 jit_solution(4437852251152108982)
XLA Ops:
  0.0 16.6 %all_gather.3 = bf16[2,2,4,32,384]{4,3,2,1,0:T(8,128)(2,1)S(1)} all-gather(bf16[2,2,1,32,384]{4,3,2,1,0:T(8,128)(2,1)} %param.12), channel_id=1, replica_groups=mesh['clips'=2,'tm'=4,'rows'=4] {'rows'}, dimensions={2}, use_global_device_ids=true | all-gather | bytes 491520 | tf_op jit(solution)/shard_map/all_gather | solution.py:215
  16.6 0.8 %copy.75 = bf16[2,2,4,32,384]{4,3,2,0,1:T(8,128)(2,1)} copy(bf16[2,2,4,32,384]{4,3,2,1,0:T(8,128)(2,1)S(1)} %all_gather.3) | data formatting | bytes 786432 | tf_op jit(solution)/shard_map/all_gather | solution.py:215
  17.4 1.3 %collective-permute-start.4 = (bf16[2,2,4,32,384]{4,3,2,0,1:T(8,128)(2,1)}, bf16[2,2,4,32,384]{4,3,2,0,1:T(8,128)(2,1)S(1)}, u32[]{:S(2)}, u32[]{:S(2)}) collective-permute-start(bf16[2,2,4,32,384]{4,3,2,0,1:T(8,128)(2,1)} %copy.75), channel_id=1, source_target_pairs={{0,4},{4,8},{8,12},{1,5},{5,9},{9,13},{2,6},{6,10},{10,14},{3,7},{... | collective-permute-start | bytes 1179656 | tf_op jit(solution)/shard_map/ppermute | solution.py:220
  18.7 0.7 broadcast_compare_fusion
  19.4 0.8 %fusion.46 = bf16[2,4,32,384]{3,2,1,0:T(8,128)(2,1)} fusion(pred[2]{0:T(512)(128)(4,1)S(1)} %broadcast_compare_fusion, bf16[2,2,4,32,384]{4,3,2,1,0:T(8,128)(2,1)S(1)} %all_gather.3), kind=kLoop, calls=%fused_computation.108 | loop fusion | flops 98304 | bytes 589826 | tf_op jit(solution)/shard_map/jit(_where)/select_n | solution.py:219
  20.2 4.0 %collective-permute-start.5 = (bf16[2,4,32,384]{3,2,1,0:T(8,128)(2,1)}, bf16[2,4,32,384]{3,2,1,0:T(8,128)(2,1)S(1)}, u32[]{:S(2)}, u32[]{:S(2)}) collective-permute-start(bf16[2,4,32,384]{3,2,1,0:T(8,128)(2,1)} %fusion.46), channel_id=1, source_target_pairs={{0,8},{4,12},{1,9},{5,13},{2,10},{6,14},{3,11},{7,15},{16,24},{20,... | collective-permute-start | bytes 589832 | tf_op jit(solution)/shard_map/ppermute | solution.py:222
  24.2 1.9 %collective-permute-start.3 = (s32[2]{0:T(128)}, s32[2]{0:T(128)}, u32[]{:S(2)}, u32[]{:S(2)}) collective-permute-start(s32[2]{0:T(128)} %bitcast.12), channel_id=1, source_target_pairs={{0,4},{4,8},{8,12},{1,5},{5,9},{9,13},{2,6},{6,10},{10,14},{3,7},{... | collective-permute-start | bytes 32 | tf_op jit(solution)/shard_map/ppermute | solution.py:221
  26.1 2.2 %collective-permute-start = (bf16[2,2,1,32,384]{4,3,1,0,2:T(8,128)(2,1)S(1)}, bf16[2,2,1,32,384]{4,3,1,0,2:T(8,128)(2,1)}, u32[]{:S(2)}, u32[]{:S(2)}) collective-permute-start(bf16[2,2,1,32,384]{4,3,1,0,2:T(8,128)(2,1)S(1)} %bitcast.130), channel_id=1, source_target_pairs={{0,1},{1,2},{2,3},{3,0},{4,5},{5,6},{6,7},{7,4},{8,9},{9,10},{10,1... | collective-permute-start | bytes 294920 | tf_op jit(solution)/shard_map/ppermute | solution.py:21
  28.4 1.2 %compare_convert_fusion = f32[2,2]{1,0:T(2,128)} fusion(s32[2]{0:T(128)} %bitcast.12), kind=kLoop, calls=%fused_computation.129 | loop fusion | flops 8 | bytes 24 | tf_op jit(solution)/shard_map/convert_element_type | solution.py:274
  29.7 5.4 %fusion.61 = (bf16[1,1,3,384,384]{4,3,2,1,0:T(8,128)(2,1)}, bf16[1,1,3,384,384]{4,3,2,1,0:T(8,128)(2,1)S(1)}, bf16[1,1,3,384,384]{4,3,2,1,0:T(8,128)(2,1)}, bf16...) fusion(bf16[3,3,3,384,384]{4,3,2,1,0:T(8,128)(2,1)} %param.15), kind=kLoop, calls=%fused_computation.138 | loop fusion | bytes 15925248 | tf_op jit(solution)/shard_map/slice | solution.py:121
  35.1 0.6 pad_clamp_fusion
  35.7 0.4 fusion.26
  36.1 1.1 %broadcast_compare_fusion.1 = pred[2]{0:T(512)(128)(4,1)} fusion(s32[2]{0:T(128)} %collective-permute-done.3), kind=kLoop, calls=%fused_computation.136 | loop fusion | flops 2 | bytes 10 | tf_op jit(solution)/shard_map/gt | solution.py:226
  37.3 6.5 %collective-permute-done.1 = bf16[2,2,1,32,384]{4,3,1,0,2:T(8,128)(2,1)S(1)} collective-permute-done((bf16[2,2,1,32,384]{4,3,1,0,2:T(8,128)(2,1)}, bf16[2,2,1,32,384]{4,3,1,0,2:T(8,128)(2,1)S(1)}, u32[]{:S(2)}, u32[]{:S(2)}) %collective-permute-start.1) | collective-permute-done | bytes 98336 | tf_op jit(solution)/shard_map/ppermute | solution.py:21
  43.8 6.4 %collective-permute-done.2 = bf16[2,2,1,32,384]{4,3,1,0,2:T(8,128)(2,1)S(1)} collective-permute-done((bf16[2,2,1,32,384]{4,3,1,0,2:T(8,128)(2,1)S(1)}, bf16[2,2,1,32,384]{4,3,1,0,2:T(8,128)(2,1)S(1)}, u32[]{:S(2)}, u32[]{:S(2)}) %collective-permute-start.2) | collective-permute-done | bytes 98336 | tf_op jit(solution)/shard_map/ppermute | solution.py:21
  50.2 1.7 %maximum_bitcast_fusion = bf16[4,2,2,32,384]{4,3,2,1,0:T(8,128)(2,1)} fusion(bf16[1,2,2,1,32,384]{5,4,2,1,0,3:T(8,128)(2,1)S(1)} %bitcast.133, bf16[1,2,2,1,32,384]{5,4,2,1,0,3:T(8,128)(2,1)S(1)} %bitcast.132, bf16[1,2,2,1,32,384]{5,4,2,1,0,3:T(8,128)(2,1)} %bitcast.3, bf16[1,2,2,1,32,384]{5,4,2,1,0,3:T(8,128)(2,1)S(1)} %bitcast.131), kind=kLoop, calls=%fused_computation.97 | loop fusion | flops 589824 | bytes 786432 | tf_op jit(solution)/shard_map/stack | solution.py:23
  51.9 1.7 %gather_fusion = bf16[4,2,2,32,384]{4,3,2,1,0:T(8,128)(2,1)S(1)} fusion(bf16[4,2,2,32,384]{4,3,2,1,0:T(8,128)(2,1)} %maximum_bitcast_fusion, s32[1024]{0:T(1024)} %pad_clamp_fusion), kind=kCustom, calls=%fused_computation | custom fusion | bytes 786448 | tf_op jit(solution)/shard_map/gather | solution.py:23
  54.0 0.3 fusion.19
  54.4 0.2 fusion.49
  54.8 3.5 %pad_slice_fusion.1 = (bf16[2,2,4,32,384]{4,3,2,1,0:T(8,128)(2,1)S(1)}, bf16[2,2,4,32,384]{4,3,2,1,0:T(8,128)(2,1)S(1)}, bf16[2,2,4,32,384]{4,3,2,1,0:T(8,128)(2...) fusion(bf16[2,4,6,32,384]{4,3,2,1,0:T(8,128)(2,1)S(1)} %fusion.6), kind=kLoop, calls=%fused_computation.38 | loop fusion | bytes 9437184 | tf_op jit(solution)/shard_map/slice | solution.py:118
  58.3 0.3 fusion.62
  58.7 0.3 pad_maximum_fusion.1
  58.9 0.9 %copy-done.8 = bf16[1,1,3,384,384]{4,3,2,1,0:T(8,128)(2,1)S(1)} copy-done((bf16[1,1,3,384,384]{4,3,2,1,0:T(8,128)(2,1)S(1)}, bf16[1,1,3,384,384]{4,3,2,1,0:T(8,128)(2,1)}, u32[]{:S(2)}) %copy-start.8) | copy-done | bytes 884760
  59.8 0.8 %fusion.64 = f32[512,384]{1,0:T(8,128)S(1)} fusion(bf16[512,1152]{1,0:T(8,128)(2,1)S(1)} %bitcast.124, bf16[1152,384]{1,0:T(8,128)(2,1)S(1)} %bitcast.125), kind=kOutput, calls=%fused_computation.141 | convolution fusion | flops 452984832 | bytes 2850816 | tf_op jit(solution)/shard_map/dot_general | solution.py:122
  60.6 0.4 pad_maximum_fusion.7
  61.0 0.7 copy-done.5
  61.8 0.8 %convolution_add_fusion.8 = f32[512,384]{1,0:T(8,128)S(1)} fusion(f32[512,384]{1,0:T(8,128)S(1)} %fusion.64, bf16[512,1152]{1,0:T(8,128)(2,1)S(1)} %bitcast.109, bf16[1152,384]{1,0:T(8,128)(2,1)S(1)} %bitcast.121), kind=kOutput, calls=%fused_computation.16 | convolution fusion | flops 453181440 | bytes 3637248 | tf_op jit(solution)/shard_map/dot_general | solution.py:122
  62.6 0.4 copy-done.4
  63.0 0.8 %convolution_add_fusion.7 = f32[512,384]{1,0:T(8,128)S(1)} fusion(f32[512,384]{1,0:T(8,128)S(1)} %convolution_add_fusion.8, bf16[512,1152]{1,0:T(8,128)(2,1)S(1)} %bitcast.110, bf16[1152,384]{1,0:T(8,128)(2,1)S(1)} %bitcast.120), kind=kOutput, calls=%fused_computation.15 | convolution fusion | flops 453181440 | bytes 3637248 | tf_op jit(solution)/shard_map/dot_general | solution.py:122
  63.8 0.3 pad_maximum_fusion.4
  64.0 0.9 %copy-done.3 = bf16[1,1,3,384,384]{4,3,2,1,0:T(8,128)(2,1)S(1)} copy-done((bf16[1,1,3,384,384]{4,3,2,1,0:T(8,128)(2,1)S(1)}, bf16[1,1,3,384,384]{4,3,2,1,0:T(8,128)(2,1)}, u32[]{:S(2)}) %copy-start.3) | copy-done | bytes 884760
  64.9 0.8 %convolution_add_fusion.6 = f32[512,384]{1,0:T(8,128)S(1)} fusion(f32[512,384]{1,0:T(8,128)S(1)} %convolution_add_fusion.7, bf16[512,1152]{1,0:T(8,128)(2,1)S(1)} %bitcast.112, bf16[1152,384]{1,0:T(8,128)(2,1)S(1)} %bitcast.119), kind=kOutput, calls=%fused_computation.14 | convolution fusion | flops 453181440 | bytes 3637248 | tf_op jit(solution)/shard_map/dot_general | solution.py:122
  65.7 0.4 copy-done.2
  66.1 0.8 %convolution_add_fusion.5 = f32[512,384]{1,0:T(8,128)S(1)} fusion(f32[512,384]{1,0:T(8,128)S(1)} %convolution_add_fusion.6, bf16[512,1152]{1,0:T(8,128)(2,1)S(1)} %bitcast.108, bf16[1152,384]{1,0:T(8,128)(2,1)S(1)} %bitcast.118), kind=kOutput, calls=%fused_computation.13 | convolution fusion | flops 453181440 | bytes 3637248 | tf_op jit(solution)/shard_map/dot_general | solution.py:122
  66.9 0.4 copy-done.1
  67.3 0.8 %convolution_add_fusion.4 = f32[512,384]{1,0:T(8,128)S(1)} fusion(f32[512,384]{1,0:T(8,128)S(1)} %convolution_add_fusion.5, bf16[512,1152]{1,0:T(8,128)(2,1)S(1)} %bitcast.111, bf16[1152,384]{1,0:T(8,128)(2,1)S(1)} %bitcast.117), kind=kOutput, calls=%fused_computation.12 | convolution fusion | flops 453181440 | bytes 3637248 | tf_op jit(solution)/shard_map/dot_general | solution.py:122
  68.1 0.3 pad_maximum_fusion.6
  68.3 0.8 %convolution_add_fusion.3 = f32[512,384]{1,0:T(8,128)S(1)} fusion(f32[512,384]{1,0:T(8,128)S(1)} %convolution_add_fusion.4, bf16[512,1152]{1,0:T(8,128)(2,1)S(1)} %bitcast.113, bf16[1152,384]{1,0:T(8,128)(2,1)S(1)} %bitcast.116), kind=kOutput, calls=%fused_computation.11 | convolution fusion | flops 453181440 | bytes 3637248 | tf_op jit(solution)/shard_map/dot_general | solution.py:122
  69.2 0.8 %convolution_add_fusion.2 = f32[512,384]{1,0:T(8,128)S(1)} fusion(f32[512,384]{1,0:T(8,128)S(1)} %convolution_add_fusion.3, bf16[512,1152]{1,0:T(8,128)(2,1)S(1)} %bitcast.107, bf16[1152,384]{1,0:T(8,128)(2,1)S(1)} %bitcast.115), kind=kOutput, calls=%fused_computation.10 | convolution fusion | flops 453181440 | bytes 3637248 | tf_op jit(solution)/shard_map/dot_general | solution.py:122
  70.0 0.3 copy-done.6
  70.3 0.8 %fusion.25 = (bf16[512,384]{1,0:T(8,128)(2,1)S(1)}, f32[512,384]{1,0:T(8,128)S(1)}) fusion(f32[2,2,4,1,32,384]{5,4,2,1,0,3:T(8,128)S(1)} %copy.88, f32[384]{0:T(512)S(1)} %copy-done.13, f32[512,384]{1,0:T(8,128)S(1)} %convolution_add_fusion.2, bf16[512,1152]{1,0:T(8,128)(2,1)S(1)} %bitcast.114, bf16[1152,384]{1,0:T(8,128)(2,1)S(1)} %bitcast.122), kind=kOutput, calls=%fused_computation.76 | convolution fusion | flops 453771264 | bytes 4818432 | tf_op jit(solution)/shard_map/dot_general | solution.py:122
  71.5 0.7 rsqrt.40
  72.3 0.2 convolution_add_fusion.10
  72.5 1.3 %convolution_add_fusion = f32[512,768]{1,0:T(8,128)S(1)} fusion(f32[768]{0:T(1024)S(1)} %slice.227, bf16[384,1152]{1,0:T(8,128)(2,1)S(1)} %copy-done.7, bf16[512,384]{1,0:T(8,128)(2,1)S(1)} %get-tuple-element.43, f32[384]{0:T(512)S(1)} %copy-done.11, f32[512]{0:T(512)} %rsqrt.40), kind=kOutput, calls=%fused_computation.5 | convolution fusion | flops 303169536 | bytes 2564096 | tf_op jit(solution)/shard_map/dot_general | solution.py:244
  73.9 0.9 %convolution_multiply_fusion = f32[4,32,128]{2,1,0:T(8,128)S(1)} fusion(f32[4,32,384]{2,1,0:T(8,128)S(1)} %bitcast.126, f32[4,128,768]{2,1,0:T(8,128)S(1)} %bitcast.105), kind=kOutput, calls=%fused_computation.36 | convolution fusion | flops 75513856 | bytes 1048576 | tf_op jit(solution)/shard_map/nqc,nkc->nqk/dot_general | solution.py:259
  75.0 0.3 convolution_convert_fusion
  75.3 0.2 fusion.9
  75.6 0.7 fusion.50
  (55 shorter events, 1.6 us)
Async XLA Ops:
  0.0 75.3 %copy-start = (bf16[384,384]{1,0:T(8,128)(2,1)S(1)}, bf16[384,384]{1,0:T(8,128)(2,1)}, u32[]{:S(2)}) copy-start(bf16[384,384]{1,0:T(8,128)(2,1)} %param.20) | copy-start | bytes 884740
  0.0 26.1 %copy-start.9 = (bf16[2,2,1,32,384]{4,3,2,1,0:T(8,128)(2,1)S(1)}, bf16[2,2,1,32,384]{4,3,2,1,0:T(8,128)(2,1)}, u32[]{:S(2)}) copy-start(bf16[2,2,1,32,384]{4,3,2,1,0:T(8,128)(2,1)} %param.11) | copy-start | bytes 294916
  0.0 28.4 %copy-start.12 = (f32[1152]{0:T(1024)S(1)}, f32[1152]{0:T(1024)}, u32[]{:S(2)}) copy-start(f32[1152]{0:T(1024)} %param.19) | copy-start | bytes 13828
  17.4 36.4 %collective-permute-start.4 = (bf16[2,2,4,32,384]{4,3,2,0,1:T(8,128)(2,1)}, bf16[2,2,4,32,384]{4,3,2,0,1:T(8,128)(2,1)S(1)}, u32[]{:S(2)}, u32[]{:S(2)}) collective-permute-start(bf16[2,2,4,32,384]{4,3,2,0,1:T(8,128)(2,1)} %copy.75), channel_id=1, source_target_pairs={{0,4},{4,8},{8,12},{1,5},{5,9},{9,13},{2,6},{6,10},{10,14},{3,7},{... | collective-permute-start | bytes 1179656 | tf_op jit(solution)/shard_map/ppermute | solution.py:220
  20.2 17.0 %collective-permute-start.5 = (bf16[2,4,32,384]{3,2,1,0:T(8,128)(2,1)}, bf16[2,4,32,384]{3,2,1,0:T(8,128)(2,1)S(1)}, u32[]{:S(2)}, u32[]{:S(2)}) collective-permute-start(bf16[2,4,32,384]{3,2,1,0:T(8,128)(2,1)} %fusion.46), channel_id=1, source_target_pairs={{0,8},{4,12},{1,9},{5,13},{2,10},{6,14},{3,11},{7,15},{16,24},{20,... | collective-permute-start | bytes 589832 | tf_op jit(solution)/shard_map/ppermute | solution.py:222
  24.2 11.9 %collective-permute-start.3 = (s32[2]{0:T(128)}, s32[2]{0:T(128)}, u32[]{:S(2)}, u32[]{:S(2)}) collective-permute-start(s32[2]{0:T(128)} %bitcast.12), channel_id=1, source_target_pairs={{0,4},{4,8},{8,12},{1,5},{5,9},{9,13},{2,6},{6,10},{10,14},{3,7},{... | collective-permute-start | bytes 32 | tf_op jit(solution)/shard_map/ppermute | solution.py:221
  26.1 11.1 %collective-permute-start = (bf16[2,2,1,32,384]{4,3,1,0,2:T(8,128)(2,1)S(1)}, bf16[2,2,1,32,384]{4,3,1,0,2:T(8,128)(2,1)}, u32[]{:S(2)}, u32[]{:S(2)}) collective-permute-start(bf16[2,2,1,32,384]{4,3,1,0,2:T(8,128)(2,1)S(1)} %bitcast.130), channel_id=1, source_target_pairs={{0,1},{1,2},{2,3},{3,0},{4,5},{5,6},{6,7},{7,4},{8,9},{9,10},{10,1... | collective-permute-start | bytes 294920 | tf_op jit(solution)/shard_map/ppermute | solution.py:21
  29.7 6.1 %copy-start.10 = (f32[384]{0:T(512)S(1)}, f32[384]{0:T(512)}, u32[]{:S(2)}) copy-start(f32[384]{0:T(512)} %param.14) | copy-start | bytes 4612
  37.2 6.6 %collective-permute-start.1 = (bf16[2,2,1,32,384]{4,3,1,0,2:T(8,128)(2,1)}, bf16[2,2,1,32,384]{4,3,1,0,2:T(8,128)(2,1)S(1)}, u32[]{:S(2)}, u32[]{:S(2)}) collective-permute-start(bf16[2,2,1,32,384]{4,3,1,0,2:T(8,128)(2,1)} %collective-permute-done), channel_id=1, source_target_pairs={{0,1},{1,2},{2,3},{3,0},{4,5},{5,6},{6,7},{7,4},{8,9},{9,10},{10,1... | collective-permute-start | bytes 294920 | tf_op jit(solution)/shard_map/ppermute | solution.py:21
  43.8 6.4 %collective-permute-start.2 = (bf16[2,2,1,32,384]{4,3,1,0,2:T(8,128)(2,1)S(1)}, bf16[2,2,1,32,384]{4,3,1,0,2:T(8,128)(2,1)S(1)}, u32[]{:S(2)}, u32[]{:S(2)}) collective-permute-start(bf16[2,2,1,32,384]{4,3,1,0,2:T(8,128)(2,1)S(1)} %collective-permute-done.1), channel_id=1, source_target_pairs={{0,1},{1,2},{2,3},{3,0},{4,5},{5,6},{6,7},{7,4},{8,9},{9,10},{10,1... | collective-permute-start | bytes 294920 | tf_op jit(solution)/shard_map/ppermute | solution.py:21
  53.7 0.6 copy-start.15
  58.7 1.2 %copy-start.8 = (bf16[1,1,3,384,384]{4,3,2,1,0:T(8,128)(2,1)S(1)}, bf16[1,1,3,384,384]{4,3,2,1,0:T(8,128)(2,1)}, u32[]{:S(2)}) copy-start(bf16[1,1,3,384,384]{4,3,2,1,0:T(8,128)(2,1)} %get-tuple-element.14) | copy-start | bytes 2654212
  60.6 1.2 %copy-start.5 = (bf16[1,1,3,384,384]{4,3,2,1,0:T(8,128)(2,1)S(1)}, bf16[1,1,3,384,384]{4,3,2,1,0:T(8,128)(2,1)}, u32[]{:S(2)}) copy-start(bf16[1,1,3,384,384]{4,3,2,1,0:T(8,128)(2,1)} %get-tuple-element.13) | copy-start | bytes 2654212
  61.8 1.2 %copy-start.4 = (bf16[1,1,3,384,384]{4,3,2,1,0:T(8,128)(2,1)S(1)}, bf16[1,1,3,384,384]{4,3,2,1,0:T(8,128)(2,1)}, u32[]{:S(2)}) copy-start(bf16[1,1,3,384,384]{4,3,2,1,0:T(8,128)(2,1)} %get-tuple-element.12) | copy-start | bytes 2654212
  63.8 1.2 %copy-start.3 = (bf16[1,1,3,384,384]{4,3,2,1,0:T(8,128)(2,1)S(1)}, bf16[1,1,3,384,384]{4,3,2,1,0:T(8,128)(2,1)}, u32[]{:S(2)}) copy-start(bf16[1,1,3,384,384]{4,3,2,1,0:T(8,128)(2,1)} %get-tuple-element.11) | copy-start | bytes 2654212
  64.9 1.2 %copy-start.2 = (bf16[1,1,3,384,384]{4,3,2,1,0:T(8,128)(2,1)S(1)}, bf16[1,1,3,384,384]{4,3,2,1,0:T(8,128)(2,1)}, u32[]{:S(2)}) copy-start(bf16[1,1,3,384,384]{4,3,2,1,0:T(8,128)(2,1)} %get-tuple-element.10) | copy-start | bytes 2654212
  66.1 1.2 %copy-start.1 = (bf16[1,1,3,384,384]{4,3,2,1,0:T(8,128)(2,1)S(1)}, bf16[1,1,3,384,384]{4,3,2,1,0:T(8,128)(2,1)}, u32[]{:S(2)}) copy-start(bf16[1,1,3,384,384]{4,3,2,1,0:T(8,128)(2,1)} %get-tuple-element.9) | copy-start | bytes 2654212
  69.1 1.2 %copy-start.6 = (bf16[1,1,3,384,384]{4,3,2,1,0:T(8,128)(2,1)S(1)}, bf16[1,1,3,384,384]{4,3,2,1,0:T(8,128)(2,1)}, u32[]{:S(2)}) copy-start(bf16[1,1,3,384,384]{4,3,2,1,0:T(8,128)(2,1)} %get-tuple-element.7) | copy-start | bytes 2654212
  69.1 1.2 %copy-start.13 = (f32[384]{0:T(512)S(1)}, f32[384]{0:T(512)}, u32[]{:S(2)}) copy-start(f32[384]{0:T(512)} %param.16) | copy-start | bytes 4612
  71.1 1.0 %copy-start.11 = (f32[384]{0:T(512)S(1)}, f32[384]{0:T(512)}, u32[]{:S(2)}) copy-start(f32[384]{0:T(512)} %param.17) | copy-start | bytes 4612
  71.1 1.2 %copy-start.7 = (bf16[384,1152]{1,0:T(8,128)(2,1)S(1)}, bf16[384,1152]{1,0:T(8,128)(2,1)}, u32[]{:S(2)}) copy-start(bf16[384,1152]{1,0:T(8,128)(2,1)} %param.18) | copy-start | bytes 2654212
  71.1 1.2 %slice-start = ((f32[1152]{0:T(1024)}), f32[384]{0:T(512)S(1)}, s32[]{:S(2)}) async-start(f32[1152]{0:T(1024)} %param.19), calls=%async_computation | async-start | bytes 4096 | tf_op jit(solution)/shard_map/slice | solution.py:257
  73.8 1.5 %copy-start.14 = (f32[384]{0:T(512)S(1)}, f32[384]{0:T(512)}, u32[]{:S(2)}) copy-start(f32[384]{0:T(512)} %param.21) | copy-start | bytes 4612
  73.9 1.7 %copy-start.16 = (f32[2,2]{1,0:T(2,128)S(1)}, f32[2,2]{1,0:T(2,128)}, u32[]{:S(2)}) copy-start(f32[2,2]{1,0:T(2,128)} %compare_convert_fusion) | copy-start | bytes 52
